TPU v7x, 128 devices: a whole 4x4x4 slice. The times are simulated.
128 devices in a mesh: req: 64 (over z, y, x), blk: 2 (over core).
Axes of the slice: x: 4, y: 4, z: 4, core: 2. Of those that a mesh axis runs over, the one named last changes fastest.
Arguments:
- normed: bfloat16 [32768, 1536], P('req', 'blk'), may hold values from -6 to 6
- router: bfloat16 [1536, 64], P('blk'), may hold values from -0.15625 to 0.15625
- adapter_down: bfloat16 [1536, 256], P('blk'), may hold values from -0.15625 to 0.15625
- adapter_up: bfloat16 [256, 1536], P(None, 'blk'), may hold values from -1.5 to 1.5
- shared_gate_up: bfloat16 [1536, 2, 1024], P(None, None, 'blk'), may hold values from -0.15625 to 0.15625
- shared_down: bfloat16 [1024, 1536], P('blk'), may hold values from -0.1875 to 0.1875
- expert_gate_up: bfloat16 [64, 1536, 1024], P('req', 'blk'), may hold values from -0.15625 to 0.15625
- expert_down: bfloat16 [64, 512, 1536], P('req', None, 'blk'), may hold values from -0.25 to 0.25
- lengths: int32 [64, 4], P('req'), may hold values from 1 to 256, 512 in all within a row
- adapter_ids: int32 [64, 4], P('req'), may hold values from 0 to 15
- routes: int32 [32768, 6], P('req'), may hold values from 0 to 63, all different within a row; in each aligned block of 512 rows (0 to 511, 512 to 1023, ...) at most 52 rows name the same one
Outputs:
- mixed: bfloat16 [32768, 1536], P('req', 'blk')
Inputs may be any that keep to these rules, and one draw needn't show every extreme that they name: `lengths`: each row of an index of req lists its 4 prompts in token order; they sum to 512, the longest is 256. `routes`: each row names 6 different experts. Among the 512 rows of one index of req no expert is named more than 52 times, a bound that some block reaches.
All inputs are finite; a program needn't handle non-finite values.
Results may differ from a plain program's by a relative error of at most 0.013.
Values may be sent and summed in bfloat16 or wider, within the bound.
No kernel may reach another device: no remote copies, remote signals or barrier semaphores. Data moves between devices by JAX's collectives and lax.ppermute only.
A program may use at most 128 MiB of HBM per device.

v0:
```python
import jax
import jax.numpy as jnp
from jax import lax
from jax.sharding import PartitionSpec as P

RANK = 16


def slot_table(target, source_row, total_slots):
    source_slot = jnp.zeros((total_slots,), jnp.int32).at[target].set(source_row)
    filled = jnp.zeros((total_slots,), jnp.int32).at[target].set(1)
    return (source_slot, filled)


def body(
    normed,
    router,
    adapter_down,
    adapter_up,
    shared_gate_up,
    shared_down,
    expert_gate_up,
    expert_down,
    lengths,
    adapter_ids,
    routes,
):
    tok_rows = normed.shape[0]
    feat_local = normed.shape[1]
    top_count = routes.shape[1]
    req_count = lax.axis_size("req")
    expert_count = req_count * expert_gate_up.shape[0]
    most_rows = (
        tok_rows * top_count + expert_count - 1
    ) // expert_count + tok_rows * top_count // (12 * expert_count)
    slot_count = req_count * most_rows
    hidden_width = expert_down.shape[1]
    logit_part = jnp.dot(normed, router, preferred_element_type=jnp.float32)
    low_part = jnp.dot(normed, adapter_down, preferred_element_type=jnp.float32)
    logits, low_all = (
        lax.psum(logit_part.astype(jnp.bfloat16), "blk").astype(jnp.float32),
        lax.psum(low_part.astype(jnp.bfloat16), "blk").astype(jnp.float32),
    )
    ends = jnp.cumsum(lengths[0])
    position = jnp.arange(tok_rows, dtype=jnp.int32)
    request = jnp.sum((position[:, None] >= ends[None, :]).astype(jnp.int32), axis=1)
    slots_req = jnp.arange(lengths.shape[1], dtype=jnp.int32)
    adapter_token = jnp.sum(
        jnp.where(request[:, None] == slots_req[None, :], adapter_ids[0][None, :], 0), axis=1
    )
    column_owner = jnp.arange(low_all.shape[1], dtype=jnp.int32) // RANK
    low = jnp.where(column_owner[None, :] == adapter_token[:, None], low_all, 0.0).astype(
        jnp.bfloat16
    )
    delta = jnp.dot(low, adapter_up, preferred_element_type=jnp.float32)
    shared_local = shared_gate_up.shape[2]
    shared_flat = shared_gate_up.reshape(shared_gate_up.shape[0], 2 * shared_local)
    shared_pre = jnp.dot(
        lax.all_gather(normed, "blk", axis=1, tiled=True),
        shared_flat,
        preferred_element_type=jnp.float32,
    )
    shared_hidden = (
        jax.nn.silu(shared_pre[:, :shared_local]) * shared_pre[:, shared_local:]
    ).astype(jnp.bfloat16)
    shared_terms = jnp.dot(shared_hidden, shared_down, preferred_element_type=jnp.float32)
    shared_out = lax.psum_scatter(
        shared_terms.astype(jnp.bfloat16), "blk", scatter_dimension=1, tiled=True
    ).astype(jnp.float32)
    scores = jax.nn.sigmoid(logits)
    chosen = jnp.take_along_axis(scores, routes, axis=1)
    gate_weight = chosen / jnp.sum(chosen, axis=1, keepdims=True)
    flat_expert = routes.reshape(-1)
    one_hot = (flat_expert[:, None] == jnp.arange(expert_count, dtype=jnp.int32)[None, :]).astype(
        jnp.int32
    )
    earlier = jnp.cumsum(one_hot, axis=0) - one_hot
    slot_rank = jnp.sum(earlier * one_hot, axis=1)
    source_row = jnp.arange(tok_rows * top_count, dtype=jnp.int32) // top_count
    weight_gate_up = expert_gate_up[0]
    weight_down = expert_down[0]
    target = flat_expert * most_rows + slot_rank
    source_slot, filled = slot_table(target, source_row, expert_count * most_rows)
    send_rows = jnp.where(filled[:, None] > 0, normed[source_slot], jnp.zeros((), jnp.bfloat16))
    received = lax.all_to_all(
        send_rows.reshape(expert_count, most_rows, feat_local),
        "req",
        split_axis=0,
        concat_axis=0,
        tiled=True,
    )
    rows_in = received.reshape(slot_count, feat_local)
    gate_up = lax.psum_scatter(
        jnp.dot(rows_in, weight_gate_up, preferred_element_type=jnp.float32).astype(jnp.bfloat16),
        "blk",
        scatter_dimension=0,
        tiled=True,
    ).astype(jnp.float32)
    hidden = (jax.nn.silu(gate_up[:, :hidden_width]) * gate_up[:, hidden_width:]).astype(
        jnp.bfloat16
    )
    expert_out = jnp.dot(
        lax.all_gather(hidden, "blk", axis=0, tiled=True),
        weight_down,
        preferred_element_type=jnp.float32,
    ).astype(jnp.bfloat16)
    returned = lax.all_to_all(
        expert_out.reshape(req_count, most_rows, feat_local),
        "req",
        split_axis=0,
        concat_axis=0,
        tiled=True,
    )
    picked = returned.reshape(expert_count * most_rows, feat_local)[target].astype(jnp.float32)
    weighted = picked * gate_weight.reshape(-1)[:, None]
    routed = jnp.sum(weighted.reshape(tok_rows, top_count, feat_local), axis=1)
    return (shared_out + 0.5 * delta + routed).astype(jnp.bfloat16)


def solution(mesh):
    return jax.shard_map(
        body,
        mesh=mesh,
        in_specs=(
            P("req", "blk"),
            P("blk", None),
            P("blk", None),
            P(None, "blk"),
            P(None, None, "blk"),
            P("blk", None),
            P("req", "blk", None),
            P("req", None, "blk"),
            P("req", None),
            P("req", None),
            P("req", None),
        ),
        out_specs=P("req", "blk"),
        check_vma=False,
    )
```

profile of v0, /device:TPU:10, one launch (start us, length us, event | category | flops | bytes accessed | tf_op | source)
XLA Modules:
  0.0 384.7 jit_solution(10369042271794032363)
XLA Ops:
  6.5 1.0 copy.34
  7.5 0.2 eq.61
  7.7 0.2 eq.57
  7.9 0.7 broadcast_multiply_fusion
  8.6 0.9 fusion.7
  9.5 32.0 %reduce-window.19 = s32[64,24,128]{2,1,0:T(8,128)S(1)} reduce-window(s32[64,24,128]{2,1,0:T(8,128)} %fusion.7, s32[]{:T(128)} %constant.58.clone.1), window={size=1x1x128 pad=0_0x0_0x127_0}, to_apply=%region_5.6 | reduce-window | flops 24969216 | bytes 1572868 | tf_op jit(solution)/shard_map/reduce-window.1
  41.5 1.2 slice.32
  42.7 1.6 copy.41
  44.2 0.2 reduce-window.20
  44.4 1.2 broadcast_add_fusion
  45.6 0.1 copy.33
  45.7 0.2 mul.54
  45.9 1.3 fusion.5
  47.3 11.8 %scatter_custom_fusion.1 = s32[3328]{0:T(1024)S(1)} fusion(s32[3072]{0:T(1024)S(1)} %bitcast.52, s32[3072]{0:T(1024)S(1)} %add_select_fusion, s32[]{:T(128)} %constant.58.clone.1), kind=kCustom, calls=%fused_computation.48 | custom fusion | bytes 13316 | tf_op jit(solution)/shard_map/scatter | solution.py:10
  59.1 10.8 %gather_fusion = bf16[3328,768]{1,0:T(8,128)(2,1)} fusion(bf16[512,768]{1,0:T(8,128)(2,1)S(1)} %copy-done.2, s32[4096]{0:T(1024)S(1)} %pad_clamp_fusion), kind=kCustom, calls=%fused_computation | custom fusion | bytes 10236928 | tf_op jit(solution)/shard_map/gather | solution.py:84
  70.0 7.4 %gather.13 = bf16[64,52,768]{2,1,0:T(8,128)(2,1)} reshape(bf16[3328,768]{1,0:T(8,128)(2,1)} %gather_fusion) | data formatting | bytes 10223616 | tf_op jit(solution)/shard_map/gather | solution.py:84
  77.3 11.8 %scatter_custom_fusion = s32[3328]{0:T(1024)S(1)} fusion(s32[3072]{0:T(1024)S(1)} %bitcast.53, s32[3072]{0:T(1024)S(1)} %broadcast.128, s32[]{:T(128)} %constant.58.clone.1), kind=kCustom, calls=%fused_computation.51 | custom fusion | bytes 13316 | tf_op jit(solution)/shard_map/scatter | solution.py:11
  89.1 0.1 broadcast_in_dim.59
  89.3 3.6 broadcast_select_fusion
  92.9 76.0 %all_to_all.10 = bf16[64,52,768]{2,1,0:T(8,128)(2,1)} all-to-all(bf16[64,52,768]{2,1,0:T(8,128)(2,1)S(1)} %broadcast_select_fusion), channel_id=1, replica_groups=mesh['req'=64,'blk'=2] {'req'}, dimensions={0} | all-to-all | bytes 10223616 | tf_op jit(solution)/shard_map/all_to_all | solution.py:85
  168.9 7.4 %reshape.143 = bf16[3328,768]{1,0:T(8,128)(2,1)} reshape(bf16[64,52,768]{2,1,0:T(8,128)(2,1)} %all_to_all.10) | data formatting | bytes 10223616 | tf_op jit(solution)/shard_map/reshape | solution.py:92
  176.3 10.0 %convolution_convert_fusion = bf16[3328,1024]{1,0:T(8,128)(2,1)} fusion(bf16[3328,768]{1,0:T(8,128)(2,1)} %reshape.143, bf16[1,768,1024]{2,1,0:T(8,128)(2,1)S(1)} %copy-done), kind=kOutput, calls=%fused_computation.6 | convolution fusion | flops 5237899264 | bytes 13500416 | tf_op jit(solution)/shard_map/dot_general | solution.py:94
  186.3 0.0 reduce-scatter.5.cloned.1.call-update
  186.3 0.2 all-gather.5.cloned.1.call-start
  186.5 16.7 %reduce-scatter.5.cloned.1.call-done = bf16[1664,1024]{1,0:T(8,128)(2,1)} async-done(((bf16[3328,1024]{1,0:T(8,128)(2,1)}), bf16[1664,1024]{1,0:T(8,128)(2,1)}) %reduce-scatter.5.cloned.1.call-update) | async-done | bytes 3407888 | tf_op jit(solution)/shard_map/reduce_scatter | solution.py:93
  203.2 2.8 convert_element_type.66
  206.0 0.0 copy-start.9
  206.0 2.4 fusion
  208.4 0.0 all-gather.5.cloned.1.call-update
  208.4 16.7 %all-gather.5.cloned.1.call-done = bf16[3328,512]{1,0:T(8,128)(2,1)} async-done(((bf16[1664,512]{1,0:T(8,128)(2,1)}), bf16[3328,512]{1,0:T(8,128)(2,1)}) %all-gather.5.cloned.1.call-update) | async-done | bytes 3407888 | tf_op jit(solution)/shard_map/all_gather | solution.py:103
  225.1 7.0 %convolution_convert_fusion.1 = bf16[3328,768]{1,0:T(8,128)(2,1)} fusion(bf16[3328,512]{1,0:T(8,128)(2,1)} %all-gather.5.cloned.1.call-done, bf16[1,512,768]{2,1,0:T(8,128)(2,1)S(1)} %copy-done.9), kind=kOutput, calls=%fused_computation.7 | convolution fusion | flops 2619801600 | bytes 9306112 | tf_op jit(solution)/shard_map/dot_general | solution.py:102
  232.2 7.4 %reshape.144 = bf16[64,52,768]{2,1,0:T(8,128)(2,1)} reshape(bf16[3328,768]{1,0:T(8,128)(2,1)} %convolution_convert_fusion.1) | data formatting | bytes 10223616 | tf_op jit(solution)/shard_map/reshape | solution.py:108
  239.6 10.7 %all-to-all-start.1 = ((bf16[64,52,768]{2,1,0:T(8,128)(2,1)}), bf16[64,52,768]{2,1,0:T(8,128)(2,1)}, u32[]{:S(2)}, u32[]{:S(2)}) async-start(bf16[64,52,768]{2,1,0:T(8,128)(2,1)} %reshape.144), calls=%async_computation.3 | async-start | bytes 11010048 | tf_op jit(solution)/shard_map/all_to_all | solution.py:107
  250.3 0.0 all-gather.3.cloned.1.call-start
  250.3 0.7 all-gather.3.cloned.1.call-update
  251.0 0.0 all-reduce.3.cloned.1.call-start
  251.1 1.0 convolution_convert_fusion.4
  252.1 1.1 convolution_convert_fusion.3
  253.2 0.0 all-reduce.3.cloned.1.call-update
  253.2 0.3 reduce-scatter.3.cloned.1.call-start
  253.5 4.5 %copy.42 = bf16[192,8,2,512]{3,1,2,0:T(8,128)(2,1)} copy(bf16[192,8,2,512]{3,2,1,0:T(2,128)(2,1)} %bitcast.47) | data formatting | bytes 6291456
  257.9 8.6 %all-gather.3.cloned.1.call-done = bf16[512,1536]{1,0:T(8,128)(2,1)} async-done(((bf16[512,768]{1,0:T(8,128)(2,1)}), bf16[512,1536]{1,0:T(8,128)(2,1)}) %all-gather.3.cloned.1.call-update) | async-done | bytes 1572880 | tf_op jit(solution)/shard_map/all_gather | solution.py:59
  266.6 4.3 %fusion.23 = f32[512,1024]{1,0:T(8,128)S(1)} fusion(bf16[512,1536]{1,0:T(8,128)(2,1)} %all-gather.3.cloned.1.call-done, bf16[1536,1024]{1,0:T(8,128)(2,1)} %bitcast.48), kind=kOutput, calls=%fused_computation.65 | convolution fusion | flops 1610612736 | bytes 6815744 | tf_op jit(solution)/shard_map/dot_general | solution.py:58
  270.9 0.0 copy-start.10
  270.9 2.2 convolution_convert_fusion.2
  273.1 0.0 reduce-scatter.3.cloned.1.call-update
  273.2 0.1 copy.38
  273.3 0.2 reshape.164
  273.5 0.2 reduce-window.18
  273.7 0.1 convert_reduce_fusion
  273.8 0.1 select_reduce_fusion
  273.9 20.4 %all-reduce.3.cloned.1.call-done = (bf16[512,64]{0,1:T(8,128)(2,1)}, bf16[512,256]{1,0:T(8,128)(2,1)}) async-done(((bf16[512,64]{0,1:T(8,128)(2,1)}, bf16[512,256]{1,0:T(8,128)(2,1)}), (bf16[512,64]{0,1:T(8,128)(2,1)}, bf16[512,256]{1,0:T(8,128)(2,1)})) %all-reduce.3.cloned.1.call-update) | async-done | bytes 327696 | tf_op jit(solution)/shard_map/psum | solution.py:41
  294.3 0.9 add_divide_fusion
  295.2 24.9 %gather_fusion.2 = f32[3072]{0:T(1024)S(1)} fusion(f32[512,64]{0,1:T(8,128)S(1)} %add_divide_fusion, s32[3072]{0:T(1024)S(1)} %reshape.164), kind=kCustom, calls=%fused_computation.2 | custom fusion | bytes 49152 | tf_op jit(solution)/shard_map/jit(take_along_axis)/gather | solution.py:71
  320.1 0.2 reshape.167
  320.3 0.1 copy.39
  320.5 0.1 copy.40
  320.6 3.3 all-to-all-done.1
  324.0 7.4 %reshape.145 = bf16[3328,768]{1,0:T(8,128)(2,1)} reshape(bf16[64,52,768]{2,1,0:T(8,128)(2,1)} %all-to-all-done.1) | data formatting | bytes 10223616 | tf_op jit(solution)/shard_map/reshape | solution.py:114
  331.4 17.7 %gather_fusion.1 = bf16[3072,768]{1,0:T(8,128)(2,1)} fusion(bf16[3328,768]{1,0:T(8,128)(2,1)} %reshape.145, s32[3072]{0:T(1024)S(1)} %broadcast_clamp_fusion), kind=kCustom, calls=%fused_computation.1 | custom fusion | bytes 9449472 | tf_op jit(solution)/shard_map/gather | solution.py:114
  349.1 9.2 %reshape.147 = f32[512,6,768]{2,1,0:T(8,128)} reshape(bf16[3072,768]{1,0:T(8,128)(2,1)} %gather_fusion.1) | data formatting | bytes 14155776 | tf_op jit(solution)/shard_map/convert_element_type | solution.py:114
  358.2 17.2 %multiply_reduce_fusion = f32[512,768]{1,0:T(8,128)S(1)} fusion(f32[512,6,768]{2,1,0:T(8,128)} %reshape.147, f32[512,6]{1,0:T(8,128)S(1)} %copy.40), kind=kLoop, calls=%fused_computation.5 | loop fusion | flops 4325376 | bytes 11022336 | tf_op jit(solution)/shard_map/reduce_sum | solution.py:116
  375.4 0.0 reduce-scatter.3.cloned.1.call-done
  375.5 2.7 add_convert_fusion
  (32 shorter events, 0.2 us)
Async XLA Ops:
  6.5 169.8 %copy-start = (bf16[1,768,1024]{2,1,0:T(8,128)(2,1)S(1)}, bf16[1,768,1024]{2,1,0:T(8,128)(2,1)}, u32[]{:S(2)}) copy-start(bf16[1,768,1024]{2,1,0:T(8,128)(2,1)} %param.17) | copy-start | bytes 4718596
  6.5 196.7 %reduce-scatter.5.cloned.1.call-start = ((), (), s32[]{:S(2)}) async-start(), calls=%async_computation.6 | async-start | bytes 10223616 | tf_op jit(solution)/shard_map/reduce_scatter | solution.py:93
  9.5 49.6 %copy-start.2 = (bf16[512,768]{1,0:T(8,128)(2,1)S(1)}, bf16[512,768]{1,0:T(8,128)(2,1)}, u32[]{:S(2)}) copy-start(bf16[512,768]{1,0:T(8,128)(2,1)} %param.11) | copy-start | bytes 2359300
  186.3 38.8 %all-gather.5.cloned.1.call-start = ((), (), s32[]{:S(2)}) async-start(), calls=%async_computation.7 | async-start | bytes 5111808 | tf_op jit(solution)/shard_map/all_gather | solution.py:103
  206.0 19.1 %copy-start.9 = (bf16[1,512,768]{2,1,0:T(8,128)(2,1)S(1)}, bf16[1,512,768]{2,1,0:T(8,128)(2,1)}, u32[]{:S(2)}) copy-start(bf16[1,512,768]{2,1,0:T(8,128)(2,1)} %param.18) | copy-start | bytes 2359300
  239.6 11.5 %copy-start.3 = (bf16[512,768]{1,0:T(8,128)(2,1)S(1)}, bf16[512,768]{1,0:T(8,128)(2,1)}, u32[]{:S(2)}) copy-start(bf16[512,768]{1,0:T(8,128)(2,1)} %param.11) | copy-start | bytes 2359300
  239.6 11.5 %copy-start.6 = (bf16[768,64]{0,1:T(8,128)(2,1)S(1)}, bf16[768,64]{0,1:T(8,128)(2,1)}, u32[]{:S(2)}) copy-start(bf16[768,64]{0,1:T(8,128)(2,1)} %param.12) | copy-start | bytes 294916
  239.6 12.5 %copy-start.5 = (bf16[768,256]{1,0:T(8,128)(2,1)S(1)}, bf16[768,256]{1,0:T(8,128)(2,1)}, u32[]{:S(2)}) copy-start(bf16[768,256]{1,0:T(8,128)(2,1)} %param.13) | copy-start | bytes 1179652
  239.6 84.4 %all-to-all-start.1 = ((bf16[64,52,768]{2,1,0:T(8,128)(2,1)}), bf16[64,52,768]{2,1,0:T(8,128)(2,1)}, u32[]{:S(2)}, u32[]{:S(2)}) async-start(bf16[64,52,768]{2,1,0:T(8,128)(2,1)} %reshape.144), calls=%async_computation.3 | async-start | bytes 11010048 | tf_op jit(solution)/shard_map/all_to_all | solution.py:107
  250.3 16.3 %all-gather.3.cloned.1.call-start = ((), (), s32[]{:S(2)}) async-start(), calls=%async_computation.4 | async-start | bytes 2359296 | tf_op jit(solution)/shard_map/all_gather | solution.py:59
  251.0 43.3 %all-reduce.3.cloned.1.call-start = ((), (), s32[]{:S(2)}) async-start(), calls=%async_computation.8 | async-start | bytes 655360 | tf_op jit(solution)/shard_map/psum | solution.py:41
  253.2 122.3 %reduce-scatter.3.cloned.1.call-start = ((), (), s32[]{:S(2)}) async-start(), calls=%async_computation.5 | async-start | bytes 2359296 | tf_op jit(solution)/shard_map/reduce_scatter | solution.py:67
  266.6 4.3 %copy-start.8 = (bf16[512,1536]{1,0:T(8,128)(2,1)S(1)}, bf16[512,1536]{1,0:T(8,128)(2,1)}, u32[]{:S(2)}) copy-start(bf16[512,1536]{1,0:T(8,128)(2,1)} %param.16) | copy-start | bytes 4718596
  270.9 2.3 copy-start.4
  270.9 2.6 copy-start.10
  270.9 2.9 copy-start.7
  358.2 19.9 %copy-start.1 = (bf16[1,768,1024]{2,1,0:T(8,128)(2,1)S(1)}, bf16[1,768,1024]{2,1,0:T(8,128)(2,1)}, u32[]{:S(2)}) copy-start(bf16[1,768,1024]{2,1,0:T(8,128)(2,1)} %param.17) | copy-start | bytes 4718596
Sparse Core Ops, SparseCore 0:
  186.4 16.7 reduce-scatter.4
  208.5 16.5 all-gather.4
  252.8 13.7 all-gather.2
  268.9 25.3 all-reduce.2
  296.5 13.0 reduce-scatter.2
where the time goes:
time: 388 us; the launch traced here: 385 us
  local copies, waits for them, and re-layouts  126 us (32%)
  blocking collectives  76 us (20%)
  waiting for transfers between devices  66.6 us (17%)
  other arithmetic  63.6 us (16%)
  matrix products  28.2 us (7%)
  between operations  13.4 us (3%)
  starting transfers between devices  11.3 us (3%)
    all_to_all x1, blocking collectives, body(): lax.all_to_all(send_rows.reshape(expert_count, most_rows, feat_local), 'r...  76 us
    another operation x4, other arithmetic  33.5 us
    gather x5, local copies, waits for them, and re-layouts, body(): chosen = jnp.take_along_axis(scores, routes, axis=1)  25.5 us
    psum x1, waiting for transfers between devices, body(): lax.psum(logit_part.astype(jnp.bfloat16), 'blk').astype(jnp.float32)  20.4 us
    gather x2, local copies, waits for them, and re-layouts, body(): normed[source_slot]  18.2 us
    gather x1, local copies, waits for them, and re-layouts, body(): returned.reshape(expert_count * most_rows, feat_local)[target]  17.7 us
    reduce_sum x1, other arithmetic, body(): routed = jnp.sum(weighted.reshape(tok_rows, top_count, feat_local), axis=1)  17.2 us
    reduce_scatter x1, waiting for transfers between devices, body(): lax.psum_scatter(jnp.dot(rows_in, weight_gate_up, preferred_element_type=...  16.7 us
  transfers between devices with their start and end apart: 6, of which 5 were waited for; matrix products, arithmetic and copies ran while one was open for 24% of the time, Pallas kernels for 0%

commit v1 on v0

--- a/solution.py
+++ b/solution.py
@@ -56,7 +56,9 @@
     shared_local = shared_gate_up.shape[2]
     shared_flat = shared_gate_up.reshape(shared_gate_up.shape[0], 2 * shared_local)
     shared_pre = jnp.dot(
-        lax.all_gather(normed, "blk", axis=1, tiled=True),
+        jnp.concatenate(
+            lax.all_to_all(jnp.stack([normed] * lax.axis_size("blk")), "blk", 0, 0), axis=1
+        ),
         shared_flat,
         preferred_element_type=jnp.float32,
     )

time: 388 us -> 372 us (0.959)
  other arithmetic: 63.6 us -> 50.4 us
    all_to_all x1, waiting for transfers between devices: 3.31 us -> 18.6 us  [body(): lax.all_to_all(expert_out.reshape(req_count, most_rows, feat_local), 'req...]
    another operation x4 -> x5, other arithmetic: 33.5 us -> 21.2 us
    all_gather x1 -> x0, waiting for transfers between devices: 8.64 us -> none  [body(): lax.all_gather(normed, 'blk', axis=1, tiled=True)]
    all_gather x1, waiting for transfers between devices: 16.7 us -> 11.3 us  [body(): lax.all_gather(hidden, 'blk', axis=0, tiled=True)]
  transfers between devices with their start and end apart: 6 -> 6, of which waited for: 5 -> 4; matrix products, arithmetic and copies ran while one was open for 24% -> 28% of each run, Pallas kernels for 0% -> 0%
where the time goes in v1:
time: 372 us; the launch traced here: 370 us
  local copies, waits for them, and re-layouts  124 us (33%)
  blocking collectives  76 us (20%)
  waiting for transfers between devices  65.7 us (18%)
  other arithmetic  50.4 us (14%)
  matrix products  26 us (7%)
  starting transfers between devices  14.7 us (4%)
  between operations  13.4 us (4%)
    all_to_all x1, blocking collectives, body(): lax.all_to_all(send_rows.reshape(expert_count, most_rows, feat_local), 'r...  76 us
    gather x5, local copies, waits for them, and re-layouts, body(): chosen = jnp.take_along_axis(scores, routes, axis=1)  25.5 us
    another operation x4, other arithmetic  19.9 us
    psum x1, waiting for transfers between devices, body(): lax.psum(logit_part.astype(jnp.bfloat16), 'blk').astype(jnp.float32)  18.8 us
    all_to_all x1, waiting for transfers between devices, body(): lax.all_to_all(expert_out.reshape(req_count, most_rows, feat_local), 'req...  18.6 us
    gather x2, local copies, waits for them, and re-layouts, body(): normed[source_slot]  18.2 us
    gather x1, local copies, waits for them, and re-layouts, body(): returned.reshape(expert_count * most_rows, feat_local)[target]  17.7 us
    reduce_sum x1, other arithmetic, body(): routed = jnp.sum(weighted.reshape(tok_rows, top_count, feat_local), axis=1)  17.2 us
  transfers between devices with their start and end apart: 6, of which 4 were waited for; matrix products, arithmetic and copies ran while one was open for 28% of the time, Pallas kernels for 0%

profile of v1, /device:TPU:10, one launch (start us, length us, event | category | flops | bytes accessed | tf_op | source)
XLA Modules:
  0.0 370.3 jit_solution(4332792420401776363)
XLA Ops:
  6.5 1.0 copy.37
  7.5 0.2 eq.61
  7.7 0.2 eq.57
  7.9 0.7 broadcast_multiply_fusion
  8.6 0.1 fusion.7
  8.7 18.3 %reduce-window.19 = s32[64,24,128]{2,1,0:T(8,128)S(1)} reduce-window(s32[64,24,128]{2,1,0:T(8,128)S(1)} %fusion.7, s32[]{:T(128)} %constant.58.clone.1), window={size=1x1x128 pad=0_0x0_0x127_0}, to_apply=%region_5.6 | reduce-window | flops 24969216 | bytes 1572868 | tf_op jit(solution)/shard_map/reduce-window.1
  27.0 1.2 slice.32
  28.2 1.6 copy.44
  29.7 0.2 reduce-window.20
  29.9 1.2 broadcast_add_fusion
  31.1 0.1 copy.36
  31.2 0.2 mul.54
  31.4 1.3 fusion.5
  32.8 11.8 %scatter_custom_fusion.1 = s32[3328]{0:T(1024)S(1)} fusion(s32[3072]{0:T(1024)S(1)} %bitcast.58, s32[3072]{0:T(1024)S(1)} %add_select_fusion, s32[]{:T(128)} %constant.58.clone.1), kind=kCustom, calls=%fused_computation.49 | custom fusion | bytes 13316 | tf_op jit(solution)/shard_map/scatter | solution.py:10
  44.6 10.8 %gather_fusion = bf16[3328,768]{1,0:T(8,128)(2,1)} fusion(bf16[512,768]{1,0:T(8,128)(2,1)S(1)} %copy-done.2, s32[4096]{0:T(1024)S(1)} %pad_clamp_fusion), kind=kCustom, calls=%fused_computation | custom fusion | bytes 10236928 | tf_op jit(solution)/shard_map/gather | solution.py:86
  55.5 7.4 %gather.13 = bf16[64,52,768]{2,1,0:T(8,128)(2,1)} reshape(bf16[3328,768]{1,0:T(8,128)(2,1)} %gather_fusion) | data formatting | bytes 10223616 | tf_op jit(solution)/shard_map/gather | solution.py:86
  62.8 11.8 %scatter_custom_fusion = s32[3328]{0:T(1024)S(1)} fusion(s32[3072]{0:T(1024)S(1)} %bitcast.59, s32[3072]{0:T(1024)S(1)} %broadcast.128, s32[]{:T(128)} %constant.58.clone.1), kind=kCustom, calls=%fused_computation.52 | custom fusion | bytes 13316 | tf_op jit(solution)/shard_map/scatter | solution.py:11
  74.6 0.1 broadcast_in_dim.59
  74.7 3.6 broadcast_select_fusion
  78.3 76.0 %all_to_all.15 = bf16[64,52,768]{2,1,0:T(8,128)(2,1)} all-to-all(bf16[64,52,768]{2,1,0:T(8,128)(2,1)S(1)} %broadcast_select_fusion), channel_id=1, replica_groups=mesh['req'=64,'blk'=2] {'req'}, dimensions={0} | all-to-all | bytes 10223616 | tf_op jit(solution)/shard_map/all_to_all | solution.py:87
  154.4 7.4 %reshape.151 = bf16[3328,768]{1,0:T(8,128)(2,1)} reshape(bf16[64,52,768]{2,1,0:T(8,128)(2,1)} %all_to_all.15) | data formatting | bytes 10223616 | tf_op jit(solution)/shard_map/reshape | solution.py:94
  161.8 10.0 %convolution_convert_fusion = bf16[3328,1024]{1,0:T(8,128)(2,1)} fusion(bf16[3328,768]{1,0:T(8,128)(2,1)} %reshape.151, bf16[1,768,1024]{2,1,0:T(8,128)(2,1)S(1)} %copy-done), kind=kOutput, calls=%fused_computation.6 | convolution fusion | flops 5237899264 | bytes 13500416 | tf_op jit(solution)/shard_map/dot_general | solution.py:96
  171.7 0.0 reduce-scatter.5.cloned.1.call-update
  171.8 0.0 all-gather.2.cloned.1.call-start
  171.8 16.9 %reduce-scatter.5.cloned.1.call-done = bf16[1664,1024]{1,0:T(8,128)(2,1)} async-done(((bf16[3328,1024]{1,0:T(8,128)(2,1)}), bf16[1664,1024]{1,0:T(8,128)(2,1)}) %reduce-scatter.5.cloned.1.call-update) | async-done | bytes 3407888 | tf_op jit(solution)/shard_map/reduce_scatter | solution.py:95
  188.7 2.8 convert_element_type.66
  191.5 2.4 fusion
  193.9 0.0 all-gather.2.cloned.1.call-update
  193.9 0.3 copy.35
  194.2 1.3 pad_maximum_fusion
  195.5 3.9 %all-to-all-start = ((bf16[2,512,768]{1,2,0:T(8,128)(2,1)}), bf16[2,512,768]{1,2,0:T(8,128)(2,1)S(1)}, u32[]{:S(2)}, u32[]{:S(2)}) async-start(bf16[2,512,768]{1,2,0:T(8,128)(2,1)} %pad_maximum_fusion), calls=%async_computation | async-start | bytes 3145728 | tf_op jit(solution)/shard_map/all_to_all | solution.py:60
  199.3 11.3 %all-gather.2.cloned.1.call-done = bf16[3328,512]{1,0:T(8,128)(2,1)} async-done(((bf16[1664,512]{1,0:T(8,128)(2,1)}), bf16[3328,512]{1,0:T(8,128)(2,1)}) %all-gather.2.cloned.1.call-update) | async-done | bytes 3407888 | tf_op jit(solution)/shard_map/all_gather | solution.py:105
  210.6 7.3 %convolution_convert_fusion.1 = bf16[3328,768]{1,0:T(8,128)(2,1)} fusion(bf16[3328,512]{1,0:T(8,128)(2,1)} %all-gather.2.cloned.1.call-done, bf16[1,512,768]{2,1,0:T(8,128)(2,1)} %param.18), kind=kOutput, calls=%fused_computation.7 | convolution fusion | flops 2619801600 | bytes 9306112 | tf_op jit(solution)/shard_map/dot_general | solution.py:104
  217.9 7.4 %reshape.152 = bf16[64,52,768]{2,1,0:T(8,128)(2,1)} reshape(bf16[3328,768]{1,0:T(8,128)(2,1)} %convolution_convert_fusion.1) | data formatting | bytes 10223616 | tf_op jit(solution)/shard_map/reshape | solution.py:110
  225.3 10.7 %all-to-all-start.2 = ((bf16[64,52,768]{2,1,0:T(8,128)(2,1)}), bf16[64,52,768]{2,1,0:T(8,128)(2,1)}, u32[]{:S(2)}, u32[]{:S(2)}) async-start(bf16[64,52,768]{2,1,0:T(8,128)(2,1)} %reshape.152), calls=%async_computation.4 | async-start | bytes 11010048 | tf_op jit(solution)/shard_map/all_to_all | solution.py:109
  236.0 0.0 all-reduce.3.cloned.1.call-start
  236.0 1.0 convolution_convert_fusion.4
  237.0 1.1 convolution_convert_fusion.3
  238.1 0.0 all-reduce.3.cloned.1.call-update
  238.1 0.0 reduce-scatter.3.cloned.1.call-start
  238.2 2.7 copy.45
  240.9 0.0 copy-start.7
  240.9 1.8 fusion.23
  242.7 0.0 copy-start.3
  242.8 2.2 convolution_convert_fusion.2
  245.0 0.0 reduce-scatter.3.cloned.1.call-update
  245.1 0.1 copy.41
  245.2 0.2 reshape.172
  245.4 0.2 reduce-window.18
  245.6 0.1 convert_reduce_fusion
  245.7 0.1 select_reduce_fusion
  245.8 18.8 %all-reduce.3.cloned.1.call-done = (bf16[512,64]{0,1:T(8,128)(2,1)}, bf16[512,256]{1,0:T(8,128)(2,1)}) async-done(((bf16[512,64]{0,1:T(8,128)(2,1)}, bf16[512,256]{1,0:T(8,128)(2,1)}), (bf16[512,64]{0,1:T(8,128)(2,1)}, bf16[512,256]{1,0:T(8,128)(2,1)})) %all-reduce.3.cloned.1.call-update) | async-done | bytes 327696 | tf_op jit(solution)/shard_map/psum | solution.py:41
  264.6 0.9 add_divide_fusion
  265.5 24.9 %gather_fusion.2 = f32[3072]{0:T(1024)S(1)} fusion(f32[512,64]{0,1:T(8,128)S(1)} %add_divide_fusion, s32[3072]{0:T(1024)S(1)} %reshape.172), kind=kCustom, calls=%fused_computation.2 | custom fusion | bytes 49152 | tf_op jit(solution)/shard_map/jit(take_along_axis)/gather | solution.py:73
  290.4 0.2 reshape.175
  290.6 0.1 copy.42
  290.8 0.1 copy.43
  290.9 18.6 %all-to-all-done.2 = bf16[64,52,768]{2,1,0:T(8,128)(2,1)} async-done(((bf16[64,52,768]{2,1,0:T(8,128)(2,1)}), bf16[64,52,768]{2,1,0:T(8,128)(2,1)}, u32[]{:S(2)}, u32[]{:S(2)}) %all-to-all-start.2) | async-done | bytes 5111840 | tf_op jit(solution)/shard_map/all_to_all | solution.py:109
  309.6 7.5 %reshape.153 = bf16[3328,768]{1,0:T(8,128)(2,1)} reshape(bf16[64,52,768]{2,1,0:T(8,128)(2,1)} %all-to-all-done.2) | data formatting | bytes 10223616 | tf_op jit(solution)/shard_map/reshape | solution.py:116
  317.0 17.7 %gather_fusion.1 = bf16[3072,768]{1,0:T(8,128)(2,1)} fusion(bf16[3328,768]{1,0:T(8,128)(2,1)} %reshape.153, s32[3072]{0:T(1024)S(1)} %broadcast_clamp_fusion), kind=kCustom, calls=%fused_computation.1 | custom fusion | bytes 9449472 | tf_op jit(solution)/shard_map/gather | solution.py:116
  334.7 9.2 %reshape.155 = f32[512,6,768]{2,1,0:T(8,128)} reshape(bf16[3072,768]{1,0:T(8,128)(2,1)} %gather_fusion.1) | data formatting | bytes 14155776 | tf_op jit(solution)/shard_map/convert_element_type | solution.py:116
  343.9 17.2 %multiply_reduce_fusion = f32[512,768]{1,0:T(8,128)S(1)} fusion(f32[512,6,768]{2,1,0:T(8,128)} %reshape.155, f32[512,6]{1,0:T(8,128)S(1)} %copy.43), kind=kLoop, calls=%fused_computation.5 | loop fusion | flops 4325376 | bytes 11022336 | tf_op jit(solution)/shard_map/reduce_sum | solution.py:118
  361.1 0.0 reduce-scatter.3.cloned.1.call-done
  361.1 2.7 add_convert_fusion
  (29 shorter events, 0.2 us)
Async XLA Ops:
  6.5 155.2 %copy-start = (bf16[1,768,1024]{2,1,0:T(8,128)(2,1)S(1)}, bf16[1,768,1024]{2,1,0:T(8,128)(2,1)}, u32[]{:S(2)}) copy-start(bf16[1,768,1024]{2,1,0:T(8,128)(2,1)} %param.17) | copy-start | bytes 4718596
  6.5 182.2 %reduce-scatter.5.cloned.1.call-start = ((), (), s32[]{:S(2)}) async-start(), calls=%async_computation.6 | async-start | bytes 10223616 | tf_op jit(solution)/shard_map/reduce_scatter | solution.py:95
  27.0 17.6 %copy-start.2 = (bf16[512,768]{1,0:T(8,128)(2,1)S(1)}, bf16[512,768]{1,0:T(8,128)(2,1)}, u32[]{:S(2)}) copy-start(bf16[512,768]{1,0:T(8,128)(2,1)} %param.11) | copy-start | bytes 2359300
  171.8 38.9 %all-gather.2.cloned.1.call-start = ((), (), s32[]{:S(2)}) async-start(), calls=%async_computation.7 | async-start | bytes 5111808 | tf_op jit(solution)/shard_map/all_gather | solution.py:105
  195.5 29.8 %all-to-all-start = ((bf16[2,512,768]{1,2,0:T(8,128)(2,1)}), bf16[2,512,768]{1,2,0:T(8,128)(2,1)S(1)}, u32[]{:S(2)}, u32[]{:S(2)}) async-start(bf16[2,512,768]{1,2,0:T(8,128)(2,1)} %pad_maximum_fusion), calls=%async_computation | async-start | bytes 3145728 | tf_op jit(solution)/shard_map/all_to_all | solution.py:60
  225.3 10.8 %copy-start.5 = (bf16[768,64]{0,1:T(8,128)(2,1)S(1)}, bf16[768,64]{0,1:T(8,128)(2,1)}, u32[]{:S(2)}) copy-start(bf16[768,64]{0,1:T(8,128)(2,1)} %param.12) | copy-start | bytes 294916
  225.3 11.8 %copy-start.4 = (bf16[768,256]{1,0:T(8,128)(2,1)S(1)}, bf16[768,256]{1,0:T(8,128)(2,1)}, u32[]{:S(2)}) copy-start(bf16[768,256]{1,0:T(8,128)(2,1)} %param.13) | copy-start | bytes 1179652
  225.3 84.3 %all-to-all-start.2 = ((bf16[64,52,768]{2,1,0:T(8,128)(2,1)}), bf16[64,52,768]{2,1,0:T(8,128)(2,1)}, u32[]{:S(2)}, u32[]{:S(2)}) async-start(bf16[64,52,768]{2,1,0:T(8,128)(2,1)} %reshape.152), calls=%async_computation.4 | async-start | bytes 11010048 | tf_op jit(solution)/shard_map/all_to_all | solution.py:109
  236.0 28.6 %all-reduce.3.cloned.1.call-start = ((), (), s32[]{:S(2)}) async-start(), calls=%async_computation.8 | async-start | bytes 655360 | tf_op jit(solution)/shard_map/psum | solution.py:41
  238.1 123.0 %reduce-scatter.3.cloned.1.call-start = ((), (), s32[]{:S(2)}) async-start(), calls=%async_computation.5 | async-start | bytes 2359296 | tf_op jit(solution)/shard_map/reduce_scatter | solution.py:69
  240.9 1.8 copy-start.7
  242.7 2.3 copy-start.3
  242.8 2.6 copy-start.8
  242.8 2.9 copy-start.6
  343.9 19.9 %copy-start.1 = (bf16[1,768,1024]{2,1,0:T(8,128)(2,1)S(1)}, bf16[1,768,1024]{2,1,0:T(8,128)(2,1)}, u32[]{:S(2)}) copy-start(bf16[1,768,1024]{2,1,0:T(8,128)(2,1)} %param.17) | copy-start | bytes 4718596
Sparse Core Ops, SparseCore 0:
  171.9 16.7 reduce-scatter.4
  194.0 16.5 all-gather.1
  239.3 25.2 all-reduce.2
  266.8 13.0 reduce-scatter.2
